TPU v7x, 256 devices: a whole 4x4x8 slice. The times are simulated.
256 devices in a mesh: tp: 8 (over x, core), ha: 8 (over y, z_lo), wa: 4 (over z_hi).
Axes of the slice: x: 4, y: 4, z: 8 (z_hi: 4, z_lo: 2; z = z_hi * 2 + z_lo), core: 2. Of those that a mesh axis runs over, the one named last changes fastest.
Arguments:
- queries: bfloat16 [1, 16, 8, 128, 3072], P(None, 'ha', 'wa', None, 'tp'), may hold values from -128 to 128
- keys: bfloat16 [1, 16, 8, 128, 3072], P(None, 'ha', 'wa', None, 'tp'), may hold values from -4.5 to 4.5
- values: bfloat16 [1, 16, 8, 128, 3072], P(None, 'ha', 'wa', None, 'tp'), may hold values from -6 to 6
- grad_out: bfloat16 [1, 16, 8, 128, 3072], P(None, 'ha', 'wa', None, 'tp'), may hold values from -6 to 6
- out_proj: bfloat16 [3072, 3072], P(('ha', 'wa'), 'tp'), may hold values from -0.109375 to 0.109375
Outputs:
- grad_queries: bfloat16 [1, 16, 8, 128, 3072], P(None, 'ha', 'wa', None, 'tp')
- grad_keys: bfloat16 [1, 16, 8, 128, 3072], P(None, 'ha', 'wa', None, 'tp')
- grad_values: bfloat16 [1, 16, 8, 128, 3072], P(None, 'ha', 'wa', None, 'tp')
All inputs are finite; a program needn't handle non-finite values.
Results may differ from a plain program's by a relative error of at most 0.014.
Values may be sent and summed in bfloat16 or wider, within the bound.
No kernel may reach another device: no remote copies, remote signals or barrier semaphores. Data moves between devices by JAX's collectives and lax.ppermute only.
A program may use at most 128 MiB of HBM per device.

v0:
```python
import jax
import jax.numpy as jnp
from jax import lax
from jax.sharding import PartitionSpec as P

HEAD = 128


def passed_along(value, axis, steps):
    count = lax.axis_size(axis)
    first, last = (max(0, -steps), min(count, count - steps))
    return lax.ppermute(value, axis, [(source, source + steps) for source in range(first, last)])


def extended_2(array, sides, width):
    for axis, dim in sides:
        peers, length = (lax.axis_size(axis), array.shape[dim])
        up = [(i, (i + 1) % peers) for i in range(peers - 1)]
        down = [(j, i) for i, j in up]
        last = lax.slice_in_dim(array, length - width, length, axis=dim)
        first = lax.slice_in_dim(array, 0, width, axis=dim)
        before = lax.ppermute(last, axis, up)
        after = lax.ppermute(first, axis, down)
        array = jnp.concatenate([before, array, after], axis=dim)
    return array


def tile_backward(query_blk, key_blk, value_blk, grad_blk, softmax_scale):
    f32 = jnp.float32
    scores = (
        jnp.einsum("qtd,qld->qtl", query_blk, key_blk, preferred_element_type=f32) * softmax_scale
    )
    scores = scores - jnp.max(scores, axis=-1, keepdims=True)
    expo = jnp.exp(scores)
    probs = expo / jnp.sum(expo, axis=-1, keepdims=True)
    probs_lo = probs.astype(jnp.bfloat16)
    attn = jnp.einsum("qtl,qld->qtd", probs_lo, value_blk, preferred_element_type=f32)
    delta = jnp.sum(grad_blk.astype(f32) * attn, axis=-1, keepdims=True)
    grad_probs = jnp.einsum("qtd,qld->qtl", grad_blk, value_blk, preferred_element_type=f32)
    grad_scores = (probs * (grad_probs - delta) * softmax_scale).astype(jnp.bfloat16)
    grad_query = jnp.einsum("qtl,qld->qtd", grad_scores, key_blk, preferred_element_type=f32)
    grad_key = jnp.einsum("qtl,qtd->qld", grad_scores, query_blk, preferred_element_type=f32)
    grad_value = jnp.einsum("qtl,qtd->qld", probs_lo, grad_blk, preferred_element_type=f32)
    return (grad_query, grad_key, grad_value)


def fold_cols(totals):
    from_left = passed_along(totals[:, :, :, -1].astype(jnp.bfloat16), "wa", 1).astype(jnp.float32)
    from_right = passed_along(totals[:, :, :, 0].astype(jnp.bfloat16), "wa", -1).astype(jnp.float32)
    inner = totals[:, :, :, 1:-1]
    inner = inner.at[:, :, :, 0].add(from_left)
    return inner.at[:, :, :, -1].add(from_right)


def fold_rows(totals):
    from_above = passed_along(totals[:, :, -1].astype(jnp.bfloat16), "ha", 1).astype(jnp.float32)
    from_below = passed_along(totals[:, :, 0].astype(jnp.bfloat16), "ha", -1).astype(jnp.float32)
    inner = totals[:, :, 1:-1]
    inner = inner.at[:, :, 0].add(from_above)
    return inner.at[:, :, -1].add(from_below)


def local(queries, keys, values, grad_out, out_proj):
    frames, tile_rows, tile_cols, tile_len, columns = queries.shape
    head_count = columns // HEAD
    whole = lax.all_gather(grad_out, "tp", axis=4, tiled=True)
    flat_rows = whole.reshape(-1, whole.shape[-1])
    grad_attn = jnp.dot(
        flat_rows,
        lax.all_gather(out_proj, ("ha", "wa"), axis=0, tiled=True),
        preferred_element_type=jnp.float32,
    )
    grad_attn = grad_attn.astype(jnp.bfloat16).reshape(queries.shape)
    stacked = jnp.stack([keys, values])
    extended = extended_2(stacked, (("ha", 2), ("wa", 3)), 1)
    row_base = lax.axis_index("ha") * tile_rows
    col_base = lax.axis_index("wa") * tile_cols
    rows_all = tile_rows * lax.axis_size("ha")
    cols_all = tile_cols * lax.axis_size("wa")
    span = min(3, frames)
    grid_f, grid_r, grid_c = jnp.meshgrid(
        jnp.arange(frames, dtype=jnp.int32),
        jnp.arange(tile_rows, dtype=jnp.int32),
        jnp.arange(tile_cols, dtype=jnp.int32),
        indexing="ij",
    )
    start_f = jnp.clip(grid_f.reshape(-1) - 1, 0, frames - span).astype(jnp.int32)
    start_r = (jnp.clip(row_base + grid_r.reshape(-1) - 1, 0, rows_all - 3) - row_base + 1).astype(
        jnp.int32
    )
    start_c = (jnp.clip(col_base + grid_c.reshape(-1) - 1, 0, cols_all - 3) - col_base + 1).astype(
        jnp.int32
    )
    tile_count = start_f.shape[0]
    zero_idx = jnp.zeros((), jnp.int32)
    softmax_scale = HEAD ** (-0.5)
    grad_q_parts = []
    total_parts = []
    for head_idx in range(head_count):
        lower = head_idx * HEAD
        both = extended[..., lower : lower + HEAD]

        def take(first, second, third):
            return lax.dynamic_slice(
                both,
                (zero_idx, first, second, third, zero_idx, zero_idx),
                (2, span, 3, 3, tile_len, HEAD),
            )

        window = jax.vmap(take)(start_f, start_r, start_c)
        key_blk = window[:, 0].reshape(tile_count, -1, HEAD)
        value_blk = window[:, 1].reshape(tile_count, -1, HEAD)
        query_blk = queries[..., lower : lower + HEAD].reshape(tile_count, tile_len, HEAD)
        grad_blk = grad_attn[..., lower : lower + HEAD].reshape(tile_count, tile_len, HEAD)
        grad_query, grad_key, grad_value = tile_backward(
            query_blk, key_blk, value_blk, grad_blk, softmax_scale
        )
        pieces = jnp.stack([grad_key, grad_value], 1).reshape(
            tile_count, 2, span, 3, 3, tile_len, HEAD
        )
        totals = jnp.zeros((2, frames, tile_rows + 2, tile_cols + 2, tile_len, HEAD), jnp.float32)

        def add_one(index, totals):
            start = (zero_idx, start_f[index], start_r[index], start_c[index], zero_idx, zero_idx)
            current = lax.dynamic_slice(totals, start, (2, span, 3, 3, tile_len, HEAD))
            return lax.dynamic_update_slice(totals, current + pieces[index], start)

        total_parts.append(lax.fori_loop(0, tile_count, add_one, totals))
        grad_q_parts.append(grad_query.reshape(frames, tile_rows, tile_cols, tile_len, HEAD))
    grad_queries = jnp.concatenate(grad_q_parts, axis=-1).astype(jnp.bfloat16)
    totals = jnp.concatenate(total_parts, axis=-1)
    folded = fold_rows(fold_cols(totals))
    return (grad_queries, folded[0].astype(jnp.bfloat16), folded[1].astype(jnp.bfloat16))


def solution(mesh):
    in_specs = (
        P(None, "ha", "wa", None, "tp"),
        P(None, "ha", "wa", None, "tp"),
        P(None, "ha", "wa", None, "tp"),
        P(None, "ha", "wa", None, "tp"),
        P(("ha", "wa"), "tp"),
    )
    out_specs = (
        P(None, "ha", "wa", None, "tp"),
        P(None, "ha", "wa", None, "tp"),
        P(None, "ha", "wa", None, "tp"),
    )
    return jax.shard_map(local, mesh=mesh, in_specs=in_specs, out_specs=out_specs, check_vma=False)
```

profile of v0, /device:TPU:64, one launch (start us, length us, event | category | flops | bytes accessed | tf_op | source)
XLA Modules:
  0.0 426.3 jit_solution(2551073699201183226)
XLA Ops:
  8.6 1.3 fusion.36
  10.0 1.3 collective-permute-start.1
  11.3 4.6 %collective-permute-start = (bf16[2,1,1,2,128,384]{5,4,0,1,3,2:T(8,128)(2,1)S(1)}, bf16[2,1,1,2,128,384]{5,4,0,1,3,2:T(8,128)(2,1)S(1)}, u32[]{:S(2)}, u32[]{:S(2)}) collective-permute-start(bf16[2,1,1,2,128,384]{5,4,0,1,3,2:T(8,128)(2,1)S(1)} %get-tuple-element.416), channel_id=1, source_target_pairs={{0,4},{4,8},{8,12},{12,16},{16,20},{20,24},{24,28},{1,5},{5,9},{9,... | collective-permute-start | bytes 1179656 | tf_op jit(solution)/shard_map/ppermute | solution.py:22
  15.8 8.0 %collective-permute-done.1 = bf16[2,1,1,2,128,384]{5,4,0,1,3,2:T(8,128)(2,1)S(1)} collective-permute-done((bf16[2,1,1,2,128,384]{5,4,0,1,3,2:T(8,128)(2,1)S(1)}, bf16[2,1,1,2,128,384]{5,4,0,1,3,2:T(8,128)(2,1)S(1)}, u32[]{:S(2)}, u32[]{:S(2)}) %collective-permute-start.1) | collective-permute-done | bytes 393248 | tf_op jit(solution)/shard_map/ppermute | solution.py:23
  23.8 1.9 collective-permute-done
  25.8 1.4 pad_maximum_fusion.5
  27.1 1.4 fusion.62
  28.5 1.9 collective-permute-start.3
  30.4 7.0 %collective-permute-start.2 = (bf16[2,1,4,1,128,384]{5,4,0,1,3,2:T(8,128)(2,1)}, bf16[2,1,4,1,128,384]{5,4,0,1,3,2:T(8,128)(2,1)S(1)}, u32[]{:S(2)}, u32[]{:S(2)}) collective-permute-start(bf16[2,1,4,1,128,384]{5,4,0,1,3,2:T(8,128)(2,1)} %get-tuple-element.412), channel_id=1, source_target_pairs={{0,1},{1,2},{2,3},{4,5},{5,6},{6,7},{8,9},{9,10},{10,11},{12,13},{... | collective-permute-start | bytes 2359304 | tf_op jit(solution)/shard_map/ppermute | solution.py:22
  37.9 1.8 fusion.63
  39.7 12.6 %collective-permute-done.3 = bf16[2,1,4,1,128,384]{5,4,0,1,3,2:T(8,128)(2,1)S(1)} collective-permute-done((bf16[2,1,4,1,128,384]{5,4,0,1,3,2:T(8,128)(2,1)}, bf16[2,1,4,1,128,384]{5,4,0,1,3,2:T(8,128)(2,1)S(1)}, u32[]{:S(2)}, u32[]{:S(2)}) %collective-permute-start.3) | collective-permute-done | bytes 786464 | tf_op jit(solution)/shard_map/ppermute | solution.py:23
  52.3 2.3 collective-permute-done.2
  56.1 2.3 gather_fusion.2
  58.4 2.3 gather_fusion.1
  61.7 3.6 fusion.61
  65.3 1.6 fusion.60
  66.8 1.6 fusion.59
  68.4 4.3 fusion.65
  72.7 2.3 fusion.66
  75.0 2.3 fusion.67
  77.3 106.3 %all-gather.5.cloned.1.call-done = bf16[3072,384]{1,0:T(8,128)(2,1)} async-done(((bf16[96,384]{1,0:T(8,128)(2,1)}), bf16[3072,384]{1,0:T(8,128)(2,1)}) %all-gather.5.cloned.1.call-update) | async-done | bytes 2359312 | tf_op jit(solution)/shard_map/all_gather | solution.py:70
  183.7 32.8 %all-gather.3.cloned.1.call-done = bf16[1,2,2,128,3072]{4,3,2,1,0:T(8,128)(2,1)} async-done(((bf16[1,2,2,128,384]{4,3,2,1,0:T(8,128)(2,1)}), bf16[1,2,2,128,3072]{4,3,2,1,0:T(8,128)(2,1)}) %all-gather.3.cloned.1.call-update) | async-done | bytes 3145744 | tf_op jit(solution)/shard_map/all_gather | solution.py:66
  216.4 4.4 %convolution_convert_fusion = bf16[512,384]{1,0:T(8,128)(2,1)S(1)} fusion(bf16[512,3072]{1,0:T(8,128)(2,1)} %bitcast.264, bf16[3072,384]{1,0:T(8,128)(2,1)} %all-gather.5.cloned.1.call-done), kind=kOutput, calls=%fused_computation.47 | convolution fusion | flops 1208156160 | bytes 5898240 | tf_op jit(solution)/shard_map/dot_general | solution.py:68
  221.6 4.0 fusion.49
  225.6 3.4 fusion.29
  229.0 3.6 fusion.52
  232.6 3.0 fusion.28
  235.7 3.6 fusion.55
  239.3 2.2 fusion.27
  241.5 2.6 fusion.21
  245.8 2.7 pad_maximum_fusion.3
  248.8 26.2 %while.45 = (s32[]{:T(128)}, f32[2,1,4,4,128,128]{5,4,3,2,1,0:T(8,128)S(1)}, s32[4]{0:T(128)S(1)}, s32[4]{0:T(128)S(1)}, f32[4,2,1,3,3,128,128]{6,5,4,3,1,2,0:T(8,128)}, /*index=5*/s32[]{:T(128)}, s32[]{:T(128)}, s32[]{:T(128)}) while((s32[]{:T(128)}, f32[2,1,4,4,128,128]{5,4,3,2,1,0:T(8,128)S(1)}, s32[4]{0:T(128)S(1)}, s32[4]{0:T(128)S(1)}, ...), condition=%wide.region_14.15_spmd, body=%wide.region_13.14_spmd.sunk | while | flops 294920 | bytes 3539141 | solution.py:128
  253.8 1.5 fusion.122
  260.4 1.5 fusion.122
  266.9 1.5 fusion.122
  273.5 1.5 fusion.122
  275.0 3.4 fusion.22
  280.5 2.7 pad_maximum_fusion.2
  283.5 26.2 %while.44 = (s32[]{:T(128)}, f32[2,1,4,4,128,128]{5,4,3,2,1,0:T(8,128)S(1)}, s32[4]{0:T(128)S(1)}, s32[4]{0:T(128)S(1)}, f32[4,2,1,3,3,128,128]{6,5,4,3,1,2,0:T(8,128)}, /*index=5*/s32[]{:T(128)}, s32[]{:T(128)}, s32[]{:T(128)}) while((s32[]{:T(128)}, f32[2,1,4,4,128,128]{5,4,3,2,1,0:T(8,128)S(1)}, s32[4]{0:T(128)S(1)}, s32[4]{0:T(128)S(1)}, ...), condition=%wide.region_12.13_spmd, body=%wide.region_11.12_spmd.sunk | while | flops 294920 | bytes 3539141 | solution.py:128
  288.5 1.5 fusion.121
  295.1 1.5 fusion.121
  301.7 1.5 fusion.121
  308.2 1.5 fusion.121
  309.7 3.3 fusion.23
  315.2 2.7 pad_maximum_fusion.1
  318.1 26.2 %while.43 = (s32[]{:T(128)}, f32[2,1,4,4,128,128]{5,4,3,2,1,0:T(8,128)S(1)}, s32[4]{0:T(128)S(1)}, s32[4]{0:T(128)S(1)}, f32[4,2,1,3,3,128,128]{6,5,4,3,1,2,0:T(8,128)}, /*index=5*/s32[]{:T(128)}, s32[]{:T(128)}, s32[]{:T(128)}) while((s32[]{:T(128)}, f32[2,1,4,4,128,128]{5,4,3,2,1,0:T(8,128)S(1)}, s32[4]{0:T(128)S(1)}, s32[4]{0:T(128)S(1)}, ...), condition=%wide.region_10.11_spmd, body=%wide.region_9.10_spmd.sunk | while | flops 294920 | bytes 3539141 | solution.py:128
  323.2 1.5 fusion.120
  329.7 1.5 fusion.120
  336.3 1.5 fusion.120
  342.8 1.5 fusion.120
  344.3 3.0 slice_bitcast_fusion.2
  347.3 5.6 %collective-permute-start.4 = (bf16[2,1,4,128,384]{4,3,0,2,1:T(8,128)(2,1)}, bf16[2,1,4,128,384]{4,3,0,2,1:T(8,128)(2,1)}, u32[]{:S(2)}, u32[]{:S(2)}) collective-permute-start(bf16[2,1,4,128,384]{4,3,0,2,1:T(8,128)(2,1)} %get-tuple-element.400), channel_id=1, source_target_pairs={{0,1},{1,2},{2,3},{4,5},{5,6},{6,7},{8,9},{9,10},{10,11},{12,13},{... | collective-permute-start | bytes 2359304 | tf_op jit(solution)/shard_map/ppermute | solution.py:12
  353.7 2.0 collective-permute-start.5
  355.7 2.2 convolution_convert_fusion.2
  358.0 2.6 pad_maximum_fusion
  361.2 26.1 %collective-permute-done.4 = bf16[2,1,4,128,384]{4,3,0,2,1:T(8,128)(2,1)} collective-permute-done((bf16[2,1,4,128,384]{4,3,0,2,1:T(8,128)(2,1)}, bf16[2,1,4,128,384]{4,3,0,2,1:T(8,128)(2,1)}, u32[]{:S(2)}, u32[]{:S(2)}) %collective-permute-start.4) | collective-permute-done | bytes 786464 | tf_op jit(solution)/shard_map/ppermute | solution.py:12
  387.3 1.3 fusion.26
  388.8 4.6 %collective-permute-done.5 = bf16[2,1,4,128,384]{4,3,0,2,1:T(8,128)(2,1)} collective-permute-done((bf16[2,1,4,128,384]{4,3,0,2,1:T(8,128)(2,1)}, bf16[2,1,4,128,384]{4,3,0,2,1:T(8,128)(2,1)}, u32[]{:S(2)}, u32[]{:S(2)}) %collective-permute-start.5) | collective-permute-done | bytes 786464 | tf_op jit(solution)/shard_map/ppermute | solution.py:12
  393.4 1.3 fusion.25
  395.9 4.1 collective-permute-start.6
  401.4 1.3 collective-permute-start.7
  402.7 1.7 pad_maximum_fusion.7
  404.5 1.8 collective-permute-done.6
  407.4 10.9 %collective-permute-done.7 = bf16[2,1,2,128,384]{4,3,2,0,1:T(8,128)(2,1)S(1)} collective-permute-done((bf16[2,1,2,128,384]{4,3,2,0,1:T(8,128)(2,1)}, bf16[2,1,2,128,384]{4,3,2,0,1:T(8,128)(2,1)S(1)}, u32[]{:S(2)}, u32[]{:S(2)}) %collective-permute-start.7) | collective-permute-done | bytes 393248 | tf_op jit(solution)/shard_map/ppermute | solution.py:12
  (118 shorter events, 32.3 us)
Async XLA Ops:
  7.2 176.5 %all-gather.5.cloned.1.call-start = ((), (), s32[]{:S(2)}) async-start(), calls=%async_computation.1 | async-start | bytes 2433024 | tf_op jit(solution)/shard_map/all_gather | solution.py:70
  7.9 208.5 %all-gather.3.cloned.1.call-start = ((), (), s32[]{:S(2)}) async-start(), calls=%async_computation | async-start | bytes 3538944 | tf_op jit(solution)/shard_map/all_gather | solution.py:66
  10.0 13.9 %collective-permute-start.1 = (bf16[2,1,1,2,128,384]{5,4,0,1,3,2:T(8,128)(2,1)S(1)}, bf16[2,1,1,2,128,384]{5,4,0,1,3,2:T(8,128)(2,1)S(1)}, u32[]{:S(2)}, u32[]{:S(2)}) collective-permute-start(bf16[2,1,1,2,128,384]{5,4,0,1,3,2:T(8,128)(2,1)S(1)} %get-tuple-element.417), channel_id=1, source_target_pairs={{4,0},{8,4},{12,8},{16,12},{20,16},{24,20},{28,24},{5,1},{9,5},{13... | collective-permute-start | bytes 1179656 | tf_op jit(solution)/shard_map/ppermute | solution.py:23
  11.3 14.5 %collective-permute-start = (bf16[2,1,1,2,128,384]{5,4,0,1,3,2:T(8,128)(2,1)S(1)}, bf16[2,1,1,2,128,384]{5,4,0,1,3,2:T(8,128)(2,1)S(1)}, u32[]{:S(2)}, u32[]{:S(2)}) collective-permute-start(bf16[2,1,1,2,128,384]{5,4,0,1,3,2:T(8,128)(2,1)S(1)} %get-tuple-element.416), channel_id=1, source_target_pairs={{0,4},{4,8},{8,12},{12,16},{16,20},{20,24},{24,28},{1,5},{5,9},{9,... | collective-permute-start | bytes 1179656 | tf_op jit(solution)/shard_map/ppermute | solution.py:22
  27.1 27.5 %copy-start.12 = (bf16[1,2,2,128,384]{4,3,2,1,0:T(8,128)(2,1)S(1)}, bf16[1,2,2,128,384]{4,3,2,1,0:T(8,128)(2,1)}, u32[]{:S(2)}) copy-start(bf16[1,2,2,128,384]{4,3,2,1,0:T(8,128)(2,1)} %param.20) | copy-start | bytes 1179652
  27.1 27.5 %copy-start.13 = (bf16[1,2,2,128,384]{4,3,2,1,0:T(8,128)(2,1)S(1)}, bf16[1,2,2,128,384]{4,3,2,1,0:T(8,128)(2,1)}, u32[]{:S(2)}) copy-start(bf16[1,2,2,128,384]{4,3,2,1,0:T(8,128)(2,1)} %param.21) | copy-start | bytes 1179652
  28.5 23.8 %collective-permute-start.3 = (bf16[2,1,4,1,128,384]{5,4,0,1,3,2:T(8,128)(2,1)}, bf16[2,1,4,1,128,384]{5,4,0,1,3,2:T(8,128)(2,1)S(1)}, u32[]{:S(2)}, u32[]{:S(2)}) collective-permute-start(bf16[2,1,4,1,128,384]{5,4,0,1,3,2:T(8,128)(2,1)} %get-tuple-element.413), channel_id=1, source_target_pairs={{1,0},{2,1},{3,2},{5,4},{6,5},{7,6},{9,8},{10,9},{11,10},{13,12},{... | collective-permute-start | bytes 2359304 | tf_op jit(solution)/shard_map/ppermute | solution.py:23
  30.4 24.2 %collective-permute-start.2 = (bf16[2,1,4,1,128,384]{5,4,0,1,3,2:T(8,128)(2,1)}, bf16[2,1,4,1,128,384]{5,4,0,1,3,2:T(8,128)(2,1)S(1)}, u32[]{:S(2)}, u32[]{:S(2)}) collective-permute-start(bf16[2,1,4,1,128,384]{5,4,0,1,3,2:T(8,128)(2,1)} %get-tuple-element.412), channel_id=1, source_target_pairs={{0,1},{1,2},{2,3},{4,5},{5,6},{6,7},{8,9},{9,10},{10,11},{12,13},{... | collective-permute-start | bytes 2359304 | tf_op jit(solution)/shard_map/ppermute | solution.py:22
  39.7 35.3 %copy-start.20 = (bf16[1,2,2,128,128]{4,3,2,1,0:T(8,128)(2,1)}, bf16[1,2,2,128,128]{4,3,2,1,0:T(8,128)(2,1)S(1)}, u32[]{:S(2)}) copy-start(bf16[1,2,2,128,128]{4,3,2,1,0:T(8,128)(2,1)S(1)} %get-tuple-element.418) | copy-start | bytes 393220
  61.7 3.6 copy-start.4
  66.8 1.6 copy-start.24
  68.4 4.3 %copy-start.10 = (bf16[4,1,1,3,3,128,128]{6,5,1,4,3,0,2:T(8,128)(2,1)S(1)}, bf16[4,1,1,3,3,128,128]{6,5,1,4,3,0,2:T(8,128)(2,1)}, u32[]{:S(2)}) copy-start(bf16[4,1,1,3,3,128,128]{6,5,1,4,3,0,2:T(8,128)(2,1)} %get-tuple-element.406) | copy-start | bytes 3538948
  68.4 4.3 %copy-start.22 = (bf16[1,2,2,128,128]{4,3,2,1,0:T(8,128)(2,1)S(1)}, bf16[1,2,2,128,128]{4,3,2,1,0:T(8,128)(2,1)}, u32[]{:S(2)}) copy-start(bf16[1,2,2,128,128]{4,3,2,1,0:T(8,128)(2,1)} %get-tuple-element.420) | copy-start | bytes 393220
  72.7 2.3 copy-start.8
  221.6 4.0 copy-start.19
  229.0 3.6 copy-start.18
  235.6 3.6 copy-start.17
  235.7 3.6 copy-start.21
  235.7 3.6 copy-start.26
  241.5 2.6 copy-start.25
  244.1 1.7 copy-start.16
  275.0 3.4 copy-start
  275.0 3.4 copy-start.23
  278.4 1.1 copy-start.5
  278.4 2.1 copy-start.15
  283.4 26.3 %copy-start.27 = (f32[4,128]{1,0:T(4,128)S(1)}, f32[4,128]{1,0:T(4,128)}, u32[]{:S(2)}) copy-start(f32[4,128]{1,0:T(4,128)} %fusion.27) | copy-start | bytes 6148
  309.7 3.4 copy-start.2
  313.1 1.0 copy-start.6
  313.1 2.1 copy-start.14
  344.3 8.7 %copy-start.11 = (bf16[4,1,1,3,3,128,128]{6,5,1,4,3,0,2:T(8,128)(2,1)S(1)}, bf16[4,1,1,3,3,128,128]{6,5,1,4,3,0,2:T(8,128)(2,1)}, u32[]{:S(2)}) copy-start(bf16[4,1,1,3,3,128,128]{6,5,1,4,3,0,2:T(8,128)(2,1)} %get-tuple-element.408) | copy-start | bytes 3538948
  347.3 39.9 %collective-permute-start.4 = (bf16[2,1,4,128,384]{4,3,0,2,1:T(8,128)(2,1)}, bf16[2,1,4,128,384]{4,3,0,2,1:T(8,128)(2,1)}, u32[]{:S(2)}, u32[]{:S(2)}) collective-permute-start(bf16[2,1,4,128,384]{4,3,0,2,1:T(8,128)(2,1)} %get-tuple-element.400), channel_id=1, source_target_pairs={{0,1},{1,2},{2,3},{4,5},{5,6},{6,7},{8,9},{9,10},{10,11},{12,13},{... | collective-permute-start | bytes 2359304 | tf_op jit(solution)/shard_map/ppermute | solution.py:12
  353.7 39.7 %collective-permute-start.5 = (bf16[2,1,4,128,384]{4,3,0,2,1:T(8,128)(2,1)}, bf16[2,1,4,128,384]{4,3,0,2,1:T(8,128)(2,1)}, u32[]{:S(2)}, u32[]{:S(2)}) collective-permute-start(bf16[2,1,4,128,384]{4,3,0,2,1:T(8,128)(2,1)} %get-tuple-element.399), channel_id=1, source_target_pairs={{1,0},{2,1},{3,2},{5,4},{6,5},{7,6},{9,8},{10,9},{11,10},{13,12},{... | collective-permute-start | bytes 2359304 | tf_op jit(solution)/shard_map/ppermute | solution.py:12
  360.9 26.4 %copy-start.1 = (f32[2,1,4,4,128,128]{5,4,3,2,1,0:T(8,128)S(1)}, f32[2,1,4,4,128,128]{5,4,3,2,1,0:T(8,128)}, u32[]{:S(2)}) copy-start(f32[2,1,4,4,128,128]{5,4,3,2,1,0:T(8,128)} %copy-done) | copy-start | bytes 6291460
  360.9 26.4 %copy-start.3 = (f32[2,1,4,4,128,128]{5,4,3,2,1,0:T(8,128)S(1)}, f32[2,1,4,4,128,128]{5,4,3,2,1,0:T(8,128)}, u32[]{:S(2)}) copy-start(f32[2,1,4,4,128,128]{5,4,3,2,1,0:T(8,128)} %copy-done.2) | copy-start | bytes 6291460
  394.7 5.3 %copy-start.7 = (bf16[4,128,1152]{1,2,0:T(8,128)(2,1)S(1)}, bf16[4,128,1152]{1,2,0:T(8,128)(2,1)}, u32[]{:S(2)}) copy-start(bf16[4,128,1152]{1,2,0:T(8,128)(2,1)} %copy-done.6) | copy-start | bytes 3538948
  394.7 5.3 %copy-start.9 = (bf16[4,1,1,3,3,128,128]{6,5,1,4,3,0,2:T(8,128)(2,1)S(1)}, bf16[4,1,1,3,3,128,128]{6,5,1,4,3,0,2:T(8,128)(2,1)}, u32[]{:S(2)}) copy-start(bf16[4,1,1,3,3,128,128]{6,5,1,4,3,0,2:T(8,128)(2,1)} %get-tuple-element.404) | copy-start | bytes 3538948
  395.9 10.3 %collective-permute-start.6 = (bf16[2,1,2,128,384]{4,3,2,0,1:T(8,128)(2,1)}, bf16[2,1,2,128,384]{4,3,2,0,1:T(8,128)(2,1)}, u32[]{:S(2)}, u32[]{:S(2)}) collective-permute-start(bf16[2,1,2,128,384]{4,3,2,0,1:T(8,128)(2,1)} %get-tuple-element.411), channel_id=1, source_target_pairs={{0,4},{4,8},{8,12},{12,16},{16,20},{20,24},{24,28},{1,5},{5,9},{9,... | collective-permute-start | bytes 1179656 | tf_op jit(solution)/shard_map/ppermute | solution.py:12
  401.4 17.0 %collective-permute-start.7 = (bf16[2,1,2,128,384]{4,3,2,0,1:T(8,128)(2,1)}, bf16[2,1,2,128,384]{4,3,2,0,1:T(8,128)(2,1)S(1)}, u32[]{:S(2)}, u32[]{:S(2)}) collective-permute-start(bf16[2,1,2,128,384]{4,3,2,0,1:T(8,128)(2,1)} %get-tuple-element.410), channel_id=1, source_target_pairs={{4,0},{8,4},{12,8},{16,12},{20,16},{24,20},{28,24},{5,1},{9,5},{13... | collective-permute-start | bytes 1179656 | tf_op jit(solution)/shard_map/ppermute | solution.py:12
Sparse Core Ops, SparseCore 0:
  9.8 173.8 all-gather.4
  185.5 30.8 all-gather.2
where the time goes:
time: 428 us; the launch traced here: 426 us
  waiting for transfers between devices  209 us (49%)
  matrix products  47.1 us (11%)
  loops' own time  46.9 us (11%)
  local copies, waits for them, and re-layouts  40.8 us (10%)
  other arithmetic  40.5 us (9%)
  starting transfers between devices  27.8 us (6%)
  between operations  14.5 us (3%)
    all_gather x1, waiting for transfers between devices, local(): lax.all_gather(out_proj, ('ha', 'wa'), axis=0, tiled=True)  106 us
    another operation x3, loops' own time, local(): total_parts.append(lax.fori_loop(0, tile_count, add_one, totals))  46.9 us
    ppermute x4, waiting for transfers between devices, passed_along(): lax.ppermute(value, axis, [(source, source + steps) for source in range(f...  43.4 us
    all_gather x1, waiting for transfers between devices, local(): whole = lax.all_gather(grad_out, 'tp', axis=4, tiled=True)  32.8 us
    ppermute x2, waiting for transfers between devices, extended_2(): after = lax.ppermute(first, axis, down)  20.6 us
    dynamic_update_slice x12, other arithmetic, add_one(): return lax.dynamic_update_slice(totals, current + pieces[index], start)  17.7 us
    ppermute x4, starting transfers between devices, passed_along(): lax.ppermute(value, axis, [(source, source + steps) for source in range(f...  13 us
    ppermute x2, starting transfers between devices, extended_2(): before = lax.ppermute(last, axis, up)  11.5 us
  transfers between devices with their start and end apart: 10, of which 10 were waited for; matrix products, arithmetic and copies ran while one was open for 10% of the time, Pallas kernels for 0%

commit v1 on v0

--- a/solution.py
+++ b/solution.py
@@ -63,7 +63,8 @@
 def local(queries, keys, values, grad_out, out_proj):
     frames, tile_rows, tile_cols, tile_len, columns = queries.shape
     head_count = columns // HEAD
-    whole = lax.all_gather(grad_out, "tp", axis=4, tiled=True)
+    copies = jnp.concatenate([grad_out] * lax.axis_size("tp"), axis=4)
+    whole = lax.all_to_all(copies, "tp", 4, 4, tiled=True)
     flat_rows = whole.reshape(-1, whole.shape[-1])
     grad_attn = jnp.dot(
         flat_rows,

time: 428 us -> 377 us (0.88)
  waiting for transfers between devices: 209 us -> 116 us
  local copies, waits for them, and re-layouts: 40.8 us -> 62.9 us
  starting transfers between devices: 27.8 us -> 43.7 us
    all_gather x1 -> x0, waiting for transfers between devices: 32.8 us -> none  [local(): whole = lax.all_gather(grad_out, 'tp', axis=4, tiled=True)]
    ppermute x4, waiting for transfers between devices: 43.4 us -> 14.7 us  [passed_along(): lax.ppermute(value, axis, [(source, source + steps) for source in range(f...]
    all_gather x1, waiting for transfers between devices: 106 us -> 90.8 us  [local(): lax.all_gather(out_proj, ('ha', 'wa'), axis=0, tiled=True)]
    ppermute x2, waiting for transfers between devices: 20.6 us -> 7.39 us  [extended_2(): after = lax.ppermute(first, axis, down)]
    ppermute x4, starting transfers between devices: 13 us -> 23.5 us  [passed_along(): lax.ppermute(value, axis, [(source, source + steps) for source in range(f...]
    all_to_all x0 -> x1, local copies, waits for them, and re-layouts: none -> 6.87 us  [local(): whole = lax.all_to_all(copies, 'tp', 4, 4, tiled=True)]
    concatenate x0 -> x2, local copies, waits for them, and re-layouts: none -> 5.78 us  [local(): copies = jnp.concatenate([grad_out] * lax.axis_size('tp'), axis=4)]
    gather x3, local copies, waits for them, and re-layouts: 5.58 us -> 10.4 us  [take(): lax.dynamic_slice(both, (zero_idx, first, second, third, zero_idx, zero_i...]
  transfers between devices with their start and end apart: 10 -> 10, of which waited for: 10 -> 9; matrix products, arithmetic and copies ran while one was open for 10% -> 18% of each run, Pallas kernels for 0% -> 0%
where the time goes in v1:
time: 377 us; the launch traced here: 375 us
  waiting for transfers between devices  116 us (31%)
  local copies, waits for them, and re-layouts  62.9 us (17%)
  matrix products  50.9 us (14%)
  loops' own time  45.3 us (12%)
  starting transfers between devices  43.7 us (12%)
  other arithmetic  41.6 us (11%)
  between operations  14.6 us (4%)
    all_gather x1, waiting for transfers between devices, local(): lax.all_gather(out_proj, ('ha', 'wa'), axis=0, tiled=True)  90.8 us
    another operation x3, loops' own time, local(): total_parts.append(lax.fori_loop(0, tile_count, add_one, totals))  45.3 us
    ppermute x4, starting transfers between devices, passed_along(): lax.ppermute(value, axis, [(source, source + steps) for source in range(f...  23.5 us
    dynamic_update_slice x12, other arithmetic, add_one(): return lax.dynamic_update_slice(totals, current + pieces[index], start)  17.7 us
    ppermute x4, waiting for transfers between devices, passed_along(): lax.ppermute(value, axis, [(source, source + steps) for source in range(f...  14.7 us
    dot_general x3, matrix products, tile_backward(): jnp.einsum('qtl,qtd->qld', probs_lo, grad_blk, preferred_element_type=f32)  11.8 us
    sub x3, matrix products, tile_backward(): scores = scores - jnp.max(scores, axis=-1, keepdims=True)  11.4 us
    ppermute x2, starting transfers between devices, extended_2(): before = lax.ppermute(last, axis, up)  11.3 us
  transfers between devices with their start and end apart: 10, of which 9 were waited for; matrix products, arithmetic and copies ran while one was open for 18% of the time, Pallas kernels for 0%

profile of v1, /device:TPU:64, one launch (start us, length us, event | category | flops | bytes accessed | tf_op | source)
XLA Modules:
  0.0 375.0 jit_solution(3443370388968799507)
XLA Ops:
  7.9 1.3 fusion.36
  9.2 1.3 collective-permute-start.1
  10.5 4.6 %collective-permute-start = (bf16[2,1,1,2,128,384]{5,4,0,1,3,2:T(8,128)(2,1)S(1)}, bf16[2,1,1,2,128,384]{5,4,0,1,3,2:T(8,128)(2,1)S(1)}, u32[]{:S(2)}, u32[]{:S(2)}) collective-permute-start(bf16[2,1,1,2,128,384]{5,4,0,1,3,2:T(8,128)(2,1)S(1)} %get-tuple-element.416), channel_id=1, source_target_pairs={{0,4},{4,8},{8,12},{12,16},{16,20},{20,24},{24,28},{1,5},{5,9},{9,... | collective-permute-start | bytes 1179656 | tf_op jit(solution)/shard_map/ppermute | solution.py:22
  16.8 6.3 %collective-permute-done.1 = bf16[2,1,1,2,128,384]{5,4,0,1,3,2:T(8,128)(2,1)S(1)} collective-permute-done((bf16[2,1,1,2,128,384]{5,4,0,1,3,2:T(8,128)(2,1)S(1)}, bf16[2,1,1,2,128,384]{5,4,0,1,3,2:T(8,128)(2,1)S(1)}, u32[]{:S(2)}, u32[]{:S(2)}) %collective-permute-start.1) | collective-permute-done | bytes 393248 | tf_op jit(solution)/shard_map/ppermute | solution.py:23
  23.7 1.3 fusion.62
  25.0 3.0 collective-permute-start.3
  28.0 6.8 %collective-permute-start.2 = (bf16[2,1,4,1,128,384]{5,4,0,1,3,2:T(8,128)(2,1)}, bf16[2,1,4,1,128,384]{5,4,0,1,3,2:T(8,128)(2,1)}, u32[]{:S(2)}, u32[]{:S(2)}) collective-permute-start(bf16[2,1,4,1,128,384]{5,4,0,1,3,2:T(8,128)(2,1)} %get-tuple-element.412), channel_id=1, source_target_pairs={{0,1},{1,2},{2,3},{4,5},{5,6},{6,7},{8,9},{9,10},{10,11},{12,13},{... | collective-permute-start | bytes 2359304 | tf_op jit(solution)/shard_map/ppermute | solution.py:22
  34.9 5.7 %copy.127 = bf16[1,2,2,128,3072]{3,2,1,0,4:T(2,128)(2,1)} copy(bf16[1,2,2,128,3072]{4,3,2,1,0:T(8,128)(2,1)S(1)} %constant_dynamic-update-slice_fusion) | data formatting | bytes 6291456 | tf_op jit(solution)/shard_map/concatenate | solution.py:66
  40.6 4.6 %all-to-all-start = ((bf16[1,2,2,128,3072]{3,2,1,0,4:T(2,128)(2,1)}), bf16[1,2,2,128,3072]{3,2,1,0,4:T(2,128)(2,1)S(1)}, u32[]{:S(2)}, u32[]{:S(2)}) async-start(bf16[1,2,2,128,3072]{3,2,1,0,4:T(2,128)(2,1)} %copy.127), calls=%async_computation | async-start | bytes 6291456 | tf_op jit(solution)/shard_map/all_to_all | solution.py:67
  47.1 1.8 fusion.63
  50.8 2.1 collective-permute-done.2
  52.8 2.0 pad_maximum_fusion.4
  54.9 2.1 fusion.58
  57.0 3.5 gather_fusion.2
  60.5 3.4 gather_fusion.1
  64.0 3.5 gather_fusion
  67.5 3.4 fusion.61
  70.9 1.6 fusion.60
  73.4 1.6 fusion.59
  75.0 4.2 %fusion.65 = (f32[4,128]{1,0:T(4,128)}, f32[4,128,1152]{1,2,0:T(8,128)}) fusion(bf16[4,1152,128]{2,1,0:T(8,128)(2,1)} %bitcast.220, bf16[4,128,128]{2,1,0:T(8,128)(2,1)S(1)} %bitcast.251), kind=kOutput, calls=%fused_computation.115 | convolution fusion | flops 152765568 | bytes 3672064 | tf_op jit(solution)/shard_map/sub | solution.py:33
  79.2 3.6 fusion.66
  82.8 3.6 fusion.67
  86.5 6.9 %copy.128 = bf16[1,2,2,128,3072]{4,3,2,1,0:T(8,128)(2,1)} copy(bf16[1,2,2,128,3072]{3,2,1,0,4:T(2,128)(2,1)S(1)} %all-to-all-done) | data formatting | bytes 6291456 | tf_op jit(solution)/shard_map/all_to_all | solution.py:67
  93.3 90.8 %all-gather.2.cloned.1.call-done = bf16[3072,384]{1,0:T(8,128)(2,1)} async-done(((bf16[96,384]{1,0:T(8,128)(2,1)}), bf16[3072,384]{1,0:T(8,128)(2,1)}) %all-gather.2.cloned.1.call-update) | async-done | bytes 2359312 | tf_op jit(solution)/shard_map/all_gather | solution.py:71
  184.2 4.4 %convolution_convert_fusion = bf16[512,384]{1,0:T(8,128)(2,1)S(1)} fusion(bf16[512,3072]{1,0:T(8,128)(2,1)} %bitcast.230, bf16[3072,384]{1,0:T(8,128)(2,1)} %all-gather.2.cloned.1.call-done), kind=kOutput, calls=%fused_computation.47 | convolution fusion | flops 1208156160 | bytes 5898240 | tf_op jit(solution)/shard_map/dot_general | solution.py:69
  188.7 3.9 %fusion.49 = f32[4,1152,128]{2,1,0:T(8,128)} fusion(bf16[4,128,128]{2,1,0:T(8,128)(2,1)S(1)} %bitcast.262, f32[4,128]{1,0:T(4,128)S(1)} %copy-done.30, bf16[4,1152,128]{2,1,0:T(8,128)(2,1)} %bitcast.221, bf16[4,128,128]{2,1,0:T(8,128)(2,1)S(1)} %bitcast.252), kind=kOutput, calls=%fused_computation.105 | convolution fusion | flops 304350848 | bytes 3803136 | tf_op jit(solution)/shard_map/qtl,qtd->qld/dot_general | solution.py:43
  192.6 2.8 fusion.29
  195.4 3.9 %fusion.52 = f32[4,1152,128]{2,1,0:T(8,128)} fusion(bf16[4,128,128]{2,1,0:T(8,128)(2,1)S(1)} %bitcast.259, f32[4,128]{1,0:T(4,128)S(1)} %get-tuple-element.426, bf16[4,1152,128]{2,1,0:T(8,128)(2,1)} %bitcast.217, bf16[4,128,128]{2,1,0:T(8,128)(2,1)S(1)} %bitcast.248), kind=kOutput, calls=%fused_computation.106 | convolution fusion | flops 304350848 | bytes 3803136 | tf_op jit(solution)/shard_map/qtl,qtd->qld/dot_general | solution.py:43
  199.3 3.3 fusion.28
  202.6 4.0 %fusion.55 = f32[4,1152,128]{2,1,0:T(8,128)} fusion(bf16[4,128,128]{2,1,0:T(8,128)(2,1)S(1)} %bitcast.256, f32[4,128]{1,0:T(4,128)S(1)} %get-tuple-element.428, bf16[4,1152,128]{2,1,0:T(8,128)(2,1)} %bitcast.213, bf16[4,128,128]{2,1,0:T(8,128)(2,1)S(1)} %bitcast.244), kind=kOutput, calls=%fused_computation.107 | convolution fusion | flops 304350848 | bytes 3803136 | tf_op jit(solution)/shard_map/qtl,qtd->qld/dot_general | solution.py:43
  206.6 3.3 fusion.27
  209.9 2.6 fusion.21
  214.2 2.7 pad_maximum_fusion.3
  217.2 24.4 %while.45 = (s32[]{:T(128)}, f32[2,1,4,4,128,128]{5,4,3,2,1,0:T(8,128)S(1)}, s32[4]{0:T(128)S(1)}, s32[4]{0:T(128)S(1)}, f32[4,2,1,3,3,128,128]{6,5,4,3,1,2,0:T(8,128)}, /*index=5*/s32[]{:T(128)}, s32[]{:T(128)}, s32[]{:T(128)}) while((s32[]{:T(128)}, f32[2,1,4,4,128,128]{5,4,3,2,1,0:T(8,128)S(1)}, s32[4]{0:T(128)S(1)}, s32[4]{0:T(128)S(1)}, ...), condition=%wide.region_14.15_spmd, body=%wide.region_13.14_spmd.sunk | while | flops 294920 | bytes 3539141 | solution.py:129
  221.8 1.5 fusion.122
  227.9 1.5 fusion.122
  234.0 1.5 fusion.122
  240.1 1.5 fusion.122
  241.6 3.4 fusion.22
  247.1 2.7 pad_maximum_fusion.2
  250.1 26.4 %while.44 = (s32[]{:T(128)}, f32[2,1,4,4,128,128]{5,4,3,2,1,0:T(8,128)S(1)}, s32[4]{0:T(128)S(1)}, s32[4]{0:T(128)S(1)}, f32[4,2,1,3,3,128,128]{6,5,4,3,1,2,0:T(8,128)}, /*index=5*/s32[]{:T(128)}, s32[]{:T(128)}, s32[]{:T(128)}) while((s32[]{:T(128)}, f32[2,1,4,4,128,128]{5,4,3,2,1,0:T(8,128)S(1)}, s32[4]{0:T(128)S(1)}, s32[4]{0:T(128)S(1)}, ...), condition=%wide.region_12.13_spmd, body=%wide.region_11.12_spmd.sunk | while | flops 294920 | bytes 3539141 | solution.py:129
  255.1 1.5 fusion.121
  261.7 1.5 fusion.121
  268.2 1.5 fusion.121
  274.8 1.5 fusion.121
  276.5 3.3 fusion.23
  282.0 2.8 pad_maximum_fusion.1
  285.0 26.2 %while.43 = (s32[]{:T(128)}, f32[2,1,4,4,128,128]{5,4,3,2,1,0:T(8,128)S(1)}, s32[4]{0:T(128)S(1)}, s32[4]{0:T(128)S(1)}, f32[4,2,1,3,3,128,128]{6,5,4,3,1,2,0:T(8,128)}, /*index=5*/s32[]{:T(128)}, s32[]{:T(128)}, s32[]{:T(128)}) while((s32[]{:T(128)}, f32[2,1,4,4,128,128]{5,4,3,2,1,0:T(8,128)S(1)}, s32[4]{0:T(128)S(1)}, s32[4]{0:T(128)S(1)}, ...), condition=%wide.region_10.11_spmd, body=%wide.region_9.10_spmd.sunk | while | flops 294920 | bytes 3539141 | solution.py:129
  290.0 1.5 fusion.120
  296.6 1.5 fusion.120
  303.2 1.5 fusion.120
  309.7 1.5 fusion.120
  311.2 3.0 slice_bitcast_fusion.2
  314.2 3.4 collective-permute-start.4
  318.3 4.2 %collective-permute-start.5 = (bf16[2,1,4,128,384]{4,3,0,2,1:T(8,128)(2,1)}, bf16[2,1,4,128,384]{4,3,0,2,1:T(8,128)(2,1)}, u32[]{:S(2)}, u32[]{:S(2)}) collective-permute-start(bf16[2,1,4,128,384]{4,3,0,2,1:T(8,128)(2,1)} %get-tuple-element.399), channel_id=1, source_target_pairs={{1,0},{2,1},{3,2},{5,4},{6,5},{7,6},{9,8},{10,9},{11,10},{13,12},{... | collective-permute-start | bytes 2359304 | tf_op jit(solution)/shard_map/ppermute | solution.py:12
  322.6 2.2 convolution_convert_fusion.2
  324.9 2.6 pad_maximum_fusion
  328.1 8.1 %collective-permute-done.4 = bf16[2,1,4,128,384]{4,3,0,2,1:T(8,128)(2,1)} collective-permute-done((bf16[2,1,4,128,384]{4,3,0,2,1:T(8,128)(2,1)}, bf16[2,1,4,128,384]{4,3,0,2,1:T(8,128)(2,1)}, u32[]{:S(2)}, u32[]{:S(2)}) %collective-permute-start.4) | collective-permute-done | bytes 786464 | tf_op jit(solution)/shard_map/ppermute | solution.py:12
  336.2 1.3 fusion.26
  338.7 1.3 fusion.25
  341.2 14.6 %collective-permute-start.6 = (bf16[2,1,2,128,384]{4,3,2,0,1:T(8,128)(2,1)}, bf16[2,1,2,128,384]{4,3,2,0,1:T(8,128)(2,1)}, u32[]{:S(2)}, u32[]{:S(2)}) collective-permute-start(bf16[2,1,2,128,384]{4,3,2,0,1:T(8,128)(2,1)} %get-tuple-element.411), channel_id=1, source_target_pairs={{0,4},{4,8},{8,12},{12,16},{16,20},{20,24},{24,28},{1,5},{5,9},{9,... | collective-permute-start | bytes 1179656 | tf_op jit(solution)/shard_map/ppermute | solution.py:12
  357.2 1.3 collective-permute-start.7
  358.5 1.7 pad_maximum_fusion.7
  361.9 5.2 %collective-permute-done.7 = bf16[2,1,2,128,384]{4,3,2,0,1:T(8,128)(2,1)S(1)} collective-permute-done((bf16[2,1,2,128,384]{4,3,2,0,1:T(8,128)(2,1)}, bf16[2,1,2,128,384]{4,3,2,0,1:T(8,128)(2,1)S(1)}, u32[]{:S(2)}, u32[]{:S(2)}) %collective-permute-start.7) | collective-permute-done | bytes 393248 | tf_op jit(solution)/shard_map/ppermute | solution.py:12
  (135 shorter events, 36.4 us)
Async XLA Ops:
  7.2 9.0 %copy-start.4 = (bf16[1,2,2,128,384]{4,3,2,1,0:T(8,128)(2,1)S(1)}, bf16[1,2,2,128,384]{4,3,2,1,0:T(8,128)(2,1)}, u32[]{:S(2)}) copy-start(bf16[1,2,2,128,384]{4,3,2,1,0:T(8,128)(2,1)} %param.22) | copy-start | bytes 1179652
  7.2 177.0 %all-gather.2.cloned.1.call-start = ((), (), s32[]{:S(2)}) async-start(), calls=%async_computation.1 | async-start | bytes 2433024 | tf_op jit(solution)/shard_map/all_gather | solution.py:71
  9.2 13.9 %collective-permute-start.1 = (bf16[2,1,1,2,128,384]{5,4,0,1,3,2:T(8,128)(2,1)S(1)}, bf16[2,1,1,2,128,384]{5,4,0,1,3,2:T(8,128)(2,1)S(1)}, u32[]{:S(2)}, u32[]{:S(2)}) collective-permute-start(bf16[2,1,1,2,128,384]{5,4,0,1,3,2:T(8,128)(2,1)S(1)} %get-tuple-element.417), channel_id=1, source_target_pairs={{4,0},{8,4},{12,8},{16,12},{20,16},{24,20},{28,24},{5,1},{9,5},{13... | collective-permute-start | bytes 1179656 | tf_op jit(solution)/shard_map/ppermute | solution.py:23
  10.5 12.9 %collective-permute-start = (bf16[2,1,1,2,128,384]{5,4,0,1,3,2:T(8,128)(2,1)S(1)}, bf16[2,1,1,2,128,384]{5,4,0,1,3,2:T(8,128)(2,1)S(1)}, u32[]{:S(2)}, u32[]{:S(2)}) collective-permute-start(bf16[2,1,1,2,128,384]{5,4,0,1,3,2:T(8,128)(2,1)S(1)} %get-tuple-element.416), channel_id=1, source_target_pairs={{0,4},{4,8},{8,12},{12,16},{16,20},{20,24},{24,28},{1,5},{5,9},{9,... | collective-permute-start | bytes 1179656 | tf_op jit(solution)/shard_map/ppermute | solution.py:22
  16.2 7.3 %copy-start.12 = (bf16[1,2,2,128,384]{4,3,2,1,0:T(8,128)(2,1)S(1)}, bf16[1,2,2,128,384]{4,3,2,1,0:T(8,128)(2,1)}, u32[]{:S(2)}) copy-start(bf16[1,2,2,128,384]{4,3,2,1,0:T(8,128)(2,1)} %param.20) | copy-start | bytes 1179652
  16.2 7.2 %copy-start.14 = (bf16[1,2,2,128,384]{4,3,2,1,0:T(8,128)(2,1)S(1)}, bf16[1,2,2,128,384]{4,3,2,1,0:T(8,128)(2,1)}, u32[]{:S(2)}) copy-start(bf16[1,2,2,128,384]{4,3,2,1,0:T(8,128)(2,1)} %param.21) | copy-start | bytes 1179652
  23.1 1.9 copy-start.18
  23.4 1.6 copy-start.19
  25.0 25.7 %collective-permute-start.3 = (bf16[2,1,4,1,128,384]{5,4,0,1,3,2:T(8,128)(2,1)}, bf16[2,1,4,1,128,384]{5,4,0,1,3,2:T(8,128)(2,1)}, u32[]{:S(2)}, u32[]{:S(2)}) collective-permute-start(bf16[2,1,4,1,128,384]{5,4,0,1,3,2:T(8,128)(2,1)} %get-tuple-element.413), channel_id=1, source_target_pairs={{1,0},{2,1},{3,2},{5,4},{6,5},{7,6},{9,8},{10,9},{11,10},{13,12},{... | collective-permute-start | bytes 2359304 | tf_op jit(solution)/shard_map/ppermute | solution.py:23
  28.0 24.8 %collective-permute-start.2 = (bf16[2,1,4,1,128,384]{5,4,0,1,3,2:T(8,128)(2,1)}, bf16[2,1,4,1,128,384]{5,4,0,1,3,2:T(8,128)(2,1)}, u32[]{:S(2)}, u32[]{:S(2)}) collective-permute-start(bf16[2,1,4,1,128,384]{5,4,0,1,3,2:T(8,128)(2,1)} %get-tuple-element.412), channel_id=1, source_target_pairs={{0,1},{1,2},{2,3},{4,5},{5,6},{6,7},{8,9},{9,10},{10,11},{12,13},{... | collective-permute-start | bytes 2359304 | tf_op jit(solution)/shard_map/ppermute | solution.py:22
  40.6 12.3 %copy-start.13 = (bf16[1,2,2,128,384]{4,3,2,1,0:T(8,128)(2,1)S(1)}, bf16[1,2,2,128,384]{4,3,2,1,0:T(8,128)(2,1)}, u32[]{:S(2)}) copy-start(bf16[1,2,2,128,384]{4,3,2,1,0:T(8,128)(2,1)} %param.20) | copy-start | bytes 1179652
  40.6 45.9 %all-to-all-start = ((bf16[1,2,2,128,3072]{3,2,1,0,4:T(2,128)(2,1)}), bf16[1,2,2,128,3072]{3,2,1,0,4:T(2,128)(2,1)S(1)}, u32[]{:S(2)}, u32[]{:S(2)}) async-start(bf16[1,2,2,128,3072]{3,2,1,0,4:T(2,128)(2,1)} %copy.127), calls=%async_computation | async-start | bytes 6291456 | tf_op jit(solution)/shard_map/all_to_all | solution.py:67
  67.5 3.4 copy-start.6
  70.9 2.5 copy-start.5
  73.4 1.6 copy-start.25
  75.0 4.2 %copy-start.24 = (bf16[1,2,2,128,128]{4,3,2,1,0:T(8,128)(2,1)S(1)}, bf16[1,2,2,128,128]{4,3,2,1,0:T(8,128)(2,1)}, u32[]{:S(2)}) copy-start(bf16[1,2,2,128,128]{4,3,2,1,0:T(8,128)(2,1)} %get-tuple-element.420) | copy-start | bytes 393220
  79.2 3.6 copy-start.23
  184.2 4.5 %copy-start.30 = (f32[4,128]{1,0:T(4,128)S(1)}, f32[4,128]{1,0:T(4,128)}, u32[]{:S(2)}) copy-start(f32[4,128]{1,0:T(4,128)} %get-tuple-element.424) | copy-start | bytes 6148
  188.7 10.6 %copy-start.29 = (bf16[1,2,2,128,128]{4,3,2,1,0:T(8,128)(2,1)}, bf16[1,2,2,128,128]{4,3,2,1,0:T(8,128)(2,1)S(1)}, u32[]{:S(2)}) copy-start(bf16[1,2,2,128,128]{4,3,2,1,0:T(8,128)(2,1)S(1)} %get-tuple-element.423) | copy-start | bytes 393220
  188.7 17.9 %copy-start.27 = (bf16[1,2,2,128,128]{4,3,2,1,0:T(8,128)(2,1)}, bf16[1,2,2,128,128]{4,3,2,1,0:T(8,128)(2,1)S(1)}, u32[]{:S(2)}) copy-start(bf16[1,2,2,128,128]{4,3,2,1,0:T(8,128)(2,1)S(1)} %get-tuple-element.421) | copy-start | bytes 393220
  188.7 3.9 %copy-start.22 = (bf16[4,1,1,3,3,128,128]{6,5,1,4,3,0,2:T(8,128)(2,1)S(1)}, bf16[4,1,1,3,3,128,128]{6,5,1,4,3,0,2:T(8,128)(2,1)}, u32[]{:S(2)}) copy-start(bf16[4,1,1,3,3,128,128]{6,5,1,4,3,0,2:T(8,128)(2,1)} %get-tuple-element.409) | copy-start | bytes 3538948
  195.4 3.9 %copy-start.21 = (bf16[4,1,1,3,3,128,128]{6,5,1,4,3,0,2:T(8,128)(2,1)S(1)}, bf16[4,1,1,3,3,128,128]{6,5,1,4,3,0,2:T(8,128)(2,1)}, u32[]{:S(2)}) copy-start(bf16[4,1,1,3,3,128,128]{6,5,1,4,3,0,2:T(8,128)(2,1)} %get-tuple-element.407) | copy-start | bytes 3538948
  202.6 4.0 %copy-start.20 = (bf16[4,1,1,3,3,128,128]{6,5,1,4,3,0,2:T(8,128)(2,1)S(1)}, bf16[4,1,1,3,3,128,128]{6,5,1,4,3,0,2:T(8,128)(2,1)}, u32[]{:S(2)}) copy-start(bf16[4,1,1,3,3,128,128]{6,5,1,4,3,0,2:T(8,128)(2,1)} %get-tuple-element.405) | copy-start | bytes 3538948
  209.9 2.6 copy-start.26
  212.5 1.7 copy-start.17
  241.6 3.4 copy-start
  245.0 1.1 copy-start.7
  245.0 2.1 copy-start.16
  250.0 26.5 %copy-start.28 = (bf16[1,2,2,128,128]{4,3,2,1,0:T(8,128)(2,1)S(1)}, bf16[1,2,2,128,128]{4,3,2,1,0:T(8,128)(2,1)}, u32[]{:S(2)}) copy-start(bf16[1,2,2,128,128]{4,3,2,1,0:T(8,128)(2,1)} %copy-done.27) | copy-start | bytes 393220
  250.0 26.5 %copy-start.31 = (f32[4,128]{1,0:T(4,128)S(1)}, f32[4,128]{1,0:T(4,128)}, u32[]{:S(2)}) copy-start(f32[4,128]{1,0:T(4,128)} %fusion.27) | copy-start | bytes 6148
  276.5 3.4 copy-start.2
  279.9 1.0 copy-start.8
  279.9 2.1 copy-start.15
  311.2 6.4 %copy-start.11 = (bf16[4,1,1,3,3,128,128]{6,5,1,4,3,0,2:T(8,128)(2,1)S(1)}, bf16[4,1,1,3,3,128,128]{6,5,1,4,3,0,2:T(8,128)(2,1)}, u32[]{:S(2)}) copy-start(bf16[4,1,1,3,3,128,128]{6,5,1,4,3,0,2:T(8,128)(2,1)} %get-tuple-element.408) | copy-start | bytes 3538948
  314.2 21.9 %collective-permute-start.4 = (bf16[2,1,4,128,384]{4,3,0,2,1:T(8,128)(2,1)}, bf16[2,1,4,128,384]{4,3,0,2,1:T(8,128)(2,1)}, u32[]{:S(2)}, u32[]{:S(2)}) collective-permute-start(bf16[2,1,4,128,384]{4,3,0,2,1:T(8,128)(2,1)} %get-tuple-element.400), channel_id=1, source_target_pairs={{0,1},{1,2},{2,3},{4,5},{5,6},{6,7},{8,9},{9,10},{10,11},{12,13},{... | collective-permute-start | bytes 2359304 | tf_op jit(solution)/shard_map/ppermute | solution.py:12
  318.3 20.4 %collective-permute-start.5 = (bf16[2,1,4,128,384]{4,3,0,2,1:T(8,128)(2,1)}, bf16[2,1,4,128,384]{4,3,0,2,1:T(8,128)(2,1)}, u32[]{:S(2)}, u32[]{:S(2)}) collective-permute-start(bf16[2,1,4,128,384]{4,3,0,2,1:T(8,128)(2,1)} %get-tuple-element.399), channel_id=1, source_target_pairs={{1,0},{2,1},{3,2},{5,4},{6,5},{7,6},{9,8},{10,9},{11,10},{13,12},{... | collective-permute-start | bytes 2359304 | tf_op jit(solution)/shard_map/ppermute | solution.py:12
  327.8 8.4 %copy-start.1 = (f32[2,1,4,4,128,128]{5,4,3,2,1,0:T(8,128)S(1)}, f32[2,1,4,4,128,128]{5,4,3,2,1,0:T(8,128)}, u32[]{:S(2)}) copy-start(f32[2,1,4,4,128,128]{5,4,3,2,1,0:T(8,128)} %copy-done) | copy-start | bytes 6291460
  327.8 8.4 %copy-start.3 = (f32[2,1,4,4,128,128]{5,4,3,2,1,0:T(8,128)S(1)}, f32[2,1,4,4,128,128]{5,4,3,2,1,0:T(8,128)}, u32[]{:S(2)}) copy-start(f32[2,1,4,4,128,128]{5,4,3,2,1,0:T(8,128)} %copy-done.2) | copy-start | bytes 6291460
  340.0 15.9 %copy-start.9 = (bf16[4,128,1152]{1,2,0:T(8,128)(2,1)S(1)}, bf16[4,128,1152]{1,2,0:T(8,128)(2,1)}, u32[]{:S(2)}) copy-start(bf16[4,128,1152]{1,2,0:T(8,128)(2,1)} %copy-done.8) | copy-start | bytes 3538948
  340.0 15.9 %copy-start.10 = (bf16[4,1,1,3,3,128,128]{6,5,1,4,3,0,2:T(8,128)(2,1)S(1)}, bf16[4,1,1,3,3,128,128]{6,5,1,4,3,0,2:T(8,128)(2,1)}, u32[]{:S(2)}) copy-start(bf16[4,1,1,3,3,128,128]{6,5,1,4,3,0,2:T(8,128)(2,1)} %get-tuple-element.404) | copy-start | bytes 3538948
  341.2 19.5 %collective-permute-start.6 = (bf16[2,1,2,128,384]{4,3,2,0,1:T(8,128)(2,1)}, bf16[2,1,2,128,384]{4,3,2,0,1:T(8,128)(2,1)}, u32[]{:S(2)}, u32[]{:S(2)}) collective-permute-start(bf16[2,1,2,128,384]{4,3,2,0,1:T(8,128)(2,1)} %get-tuple-element.411), channel_id=1, source_target_pairs={{0,4},{4,8},{8,12},{12,16},{16,20},{20,24},{24,28},{1,5},{5,9},{9,... | collective-permute-start | bytes 1179656 | tf_op jit(solution)/shard_map/ppermute | solution.py:12
  357.2 9.9 %collective-permute-start.7 = (bf16[2,1,2,128,384]{4,3,2,0,1:T(8,128)(2,1)}, bf16[2,1,2,128,384]{4,3,2,0,1:T(8,128)(2,1)S(1)}, u32[]{:S(2)}, u32[]{:S(2)}) collective-permute-start(bf16[2,1,2,128,384]{4,3,2,0,1:T(8,128)(2,1)} %get-tuple-element.410), channel_id=1, source_target_pairs={{4,0},{8,4},{12,8},{16,12},{20,16},{24,20},{28,24},{5,1},{9,5},{13... | collective-permute-start | bytes 1179656 | tf_op jit(solution)/shard_map/ppermute | solution.py:12
Sparse Core Ops, SparseCore 0:
  9.8 174.3 all-gather.1
